TPU v7x, 512 devices: a whole 4x4x16 slice. The times are simulated.
512 devices in a mesh: pipe: 16 (over z_hi, y), zero: 32 (over z_lo, x, core).
Axes of the slice: x: 4, y: 4, z: 16 (z_hi: 4, z_lo: 4; z = z_hi * 4 + z_lo), core: 2. Of those that a mesh axis runs over, the one named last changes fastest.
Arguments:
- residual: bfloat16 [16, 2048, 4096], P('pipe', 'zero'), may hold values from -6 to 6
- norm_gain: bfloat16 [16, 4096], P('pipe'), may hold values from 0.099609375 to 1.8984375
- queries: bfloat16 [16, 2048, 4096], P('pipe', 'zero'), may hold values from -74 to 74
- cached_kv: bfloat16 [16, 512, 1024], P('pipe', 'zero'), may hold values from -6 to 6
- panel_blocks: bfloat16 [16, 160, 128, 128], P('pipe', 'zero'), may hold values from -0.125 to 0.125
- block_rows: int32 [16, 8, 20], P('pipe'), may hold values from 0 to 31, as said below
- counts: int32 [16, 8], P('pipe'), may hold values from 12 to 20, as said below
Outputs:
- passed: bfloat16 [16, 2048, 4096], P('pipe', 'zero')
- new_kv: bfloat16 [16, 2048, 1024], P('pipe', 'zero')
Inputs may be any that keep to these rules, and one draw needn't show every extreme that they name: `block_rows`: row blocks named by the slots of one panel are all different. `counts`: slots at or beyond a panel's count are padding.
All inputs are finite; a program needn't handle non-finite values.
Results may differ from a plain program's by a relative error of at most 0.0047.
The roundings to bfloat16 on the way count: a program that leaves them out, or rounds other values in their place, can miss the bound.
Values may be sent and summed in bfloat16 or wider, within the bound.
No kernel may reach another device: no remote copies, remote signals or barrier semaphores. Data moves between devices by JAX's collectives and lax.ppermute only.
A program may use at most 64 MiB of HBM per device.

v0:
```python
import math
import jax
import jax.numpy as jnp
from jax import lax
from jax.sharding import PartitionSpec as P

QH = 32
KVH = 4
HD = 128


def passed_along(block, axis, distance):
    devices = range(lax.axis_size(axis))
    route = [((i - distance) % len(devices), i) for i in devices]
    return lax.ppermute(block, axis, route)


def local(residual, norm_gain, queries, cached_kv, panel_blocks, block_rows, counts):
    row_count = residual.shape[1]
    model_width = residual.shape[2]
    zero_index = lax.axis_index("zero")
    stream = residual[0].astype(jnp.float32)
    normed = (
        stream
        * lax.rsqrt(jnp.mean(stream * stream, axis=-1, keepdims=True) + 1e-05)
        * norm_gain[0].astype(jnp.float32)
    ).astype(jnp.bfloat16)
    block_size = panel_blocks.shape[-1]
    panels = block_rows.shape[1]
    slot_depth = block_rows.shape[2]
    row_table = block_rows[0].reshape(-1)
    slot_live = (
        (jnp.arange(slot_depth)[None, :] < counts[0][:, None]).astype(jnp.float32).reshape(-1)
    )
    normed_grid = normed.reshape(row_count, model_width // block_size, block_size)
    kv_heads = KVH
    head_size = HD
    group_size = QH // KVH
    kv_width = kv_heads * head_size
    score_scale = 1.0 / math.sqrt(head_size)
    query_grid = queries[0].reshape(row_count, kv_heads, group_size, head_size)
    first_query = zero_index * row_count
    query_pos = first_query + jnp.arange(row_count)
    initial = (
        jnp.full((kv_heads, row_count, group_size), -1e30, jnp.float32),
        jnp.zeros((kv_heads, row_count, group_size), jnp.float32),
        jnp.zeros((kv_heads, row_count, group_size, head_size), jnp.float32),
    )

    def absorb(running, portion, visible):
        run_max, run_sum, run_acc = running
        key_count = portion.shape[0]
        key_grid = portion[:, :kv_width].reshape(key_count, kv_heads, head_size)
        value_grid = portion[:, kv_width:].reshape(key_count, kv_heads, head_size)
        scores = (
            jnp.einsum("rgjd,ngd->grjn", query_grid, key_grid, preferred_element_type=jnp.float32)
            * score_scale
        )
        visible_mask = visible[None, :, None, :]
        new_max = jnp.maximum(run_max, jnp.max(jnp.where(visible_mask, scores, -1e30), axis=-1))
        shrink = jnp.exp(run_max - new_max)
        weights = jnp.where(visible_mask, jnp.exp(scores - new_max[..., None]), 0.0)
        new_sum = run_sum * shrink + jnp.sum(weights, axis=-1)
        new_acc = run_acc * shrink[..., None] + jnp.einsum(
            "grjn,ngd->grjd",
            weights.astype(jnp.bfloat16),
            value_grid,
            preferred_element_type=jnp.float32,
        )
        return (new_max, new_sum, new_acc)

    chosen = jnp.take(normed_grid, row_table, axis=1)
    slot_terms = jnp.einsum(
        "rsk,skn->rsn",
        chosen,
        lax.all_gather(panel_blocks[0], "zero", axis=0, tiled=True),
        preferred_element_type=jnp.float32,
    )
    slot_terms = slot_terms * slot_live[None, :, None]
    summed = slot_terms.reshape(row_count, panels, slot_depth, block_size).sum(axis=2)
    kv_new = summed.reshape(row_count, panels * block_size).astype(jnp.bfloat16)
    cache_portion = lax.all_gather(cached_kv[0], "zero", axis=0, tiled=True)
    softmax_state = absorb(
        initial, cache_portion, jnp.ones((row_count, cache_portion.shape[0]), bool)
    )
    portion = lax.all_gather(kv_new, "zero", axis=0, tiled=True)
    key_pos = jnp.arange(portion.shape[0])
    visible = key_pos[None, :] <= query_pos[:, None]
    softmax_state = lax.cond(
        jnp.int32(0) <= first_query + row_count - 1,
        lambda state_in: absorb(state_in, portion, visible),
        lambda state_in: state_in,
        softmax_state,
    )
    run_max, denominator, run_acc = softmax_state
    attended = run_acc / denominator[..., None]
    attended = jnp.transpose(attended, (1, 0, 2, 3)).reshape(
        row_count, kv_heads * group_size * head_size
    )
    updated = (stream + attended).astype(jnp.bfloat16)
    passed = passed_along(updated[None], "pipe", 1)
    return (passed, kv_new[None])


def solution(mesh):
    in_specs = (
        P("pipe", "zero", None),
        P("pipe", None),
        P("pipe", "zero", None),
        P("pipe", "zero", None),
        P("pipe", "zero", None, None),
        P("pipe", None, None),
        P("pipe", None),
    )
    out_specs = (P("pipe", "zero", None), P("pipe", "zero", None))
    return jax.shard_map(local, mesh=mesh, in_specs=in_specs, out_specs=out_specs, check_vma=False)
```

profile of v0, /device:TPU:96, one launch (start us, length us, event | category | flops | bytes accessed | tf_op | source)
XLA Modules:
  0.0 306.2 jit_solution(14598807501692515659)
XLA Ops:
  8.7 1.1 convert_bitcast_fusion
  9.8 0.7 fusion.37
  10.6 0.8 reshape_squeeze.10
  11.3 0.8 reshape_squeeze.9
  12.2 0.7 mul.79
  14.1 1.1 gather_fusion
  15.1 66.1 %all-gather.10.cloned.1.call-done = bf16[1,160,128,128]{3,2,0,1:T(8,128)(2,1)} async-done(((bf16[1,5,128,128]{3,2,0,1:T(8,128)(2,1)}), bf16[1,160,128,128]{3,2,0,1:T(8,128)(2,1)}) %all-gather.10.cloned.1.call-update) | async-done | bytes 5242896 | tf_op jit(solution)/shard_map/all_gather | solution.py:76
  81.3 6.4 %broadcast_multiply_fusion = f32[160,64,128]{2,1,0:T(8,128)} fusion(f32[160]{0:T(256)S(1)} %reshape.131, bf16[1,160,128,128]{3,2,0,1:T(8,128)(2,1)} %all-gather.10.cloned.1.call-done, bf16[160,64,128]{2,1,0:T(8,128)(2,1)S(1)} %gather_fusion, pred[160]{0:T(512)(128)(4,1)S(1)} %compare_and_fusion), kind=kOutput, calls=%fused_computation.24 | convolution fusion | flops 338165760 | bytes 13108000 | tf_op jit(solution)/shard_map/rsk,skn->rsn/dot_general | solution.py:73
  87.7 3.0 reduce_sum.38
  91.5 54.7 %all-gather.8.cloned.1.call-done = bf16[1,512,1024]{2,1,0:T(8,128)(2,1)} async-done(((bf16[1,16,1024]{2,1,0:T(8,128)(2,1)}), bf16[1,512,1024]{2,1,0:T(8,128)(2,1)}) %all-gather.8.cloned.1.call-update) | async-done | bytes 1048592 | tf_op jit(solution)/shard_map/all_gather | solution.py:82
  146.2 1.5 copy.42
  147.7 0.8 multiply_reduce_fusion
  148.5 1.3 fusion.15
  149.9 1.5 fusion.27
  151.3 64.2 %all-gather.6.cloned.1.call-done = bf16[2048,1024]{1,0:T(8,128)(2,1)} async-done(((bf16[64,1024]{1,0:T(8,128)(2,1)}), bf16[2048,1024]{1,0:T(8,128)(2,1)}) %all-gather.6.cloned.1.call-update) | async-done | bytes 4194320 | tf_op jit(solution)/shard_map/all_gather | solution.py:86
  215.6 26.3 %conditional.1 = ((f32[4,64,8]{2,1,0:T(8,128)S(1)}, f32[4,64,8,128]{3,2,1,0:T(8,128)S(1)})) conditional(s32[]{:T(128)} %convert_element_type.57, (f32[4,64,8]{2,1,0:T(8,128)S(1)}, f32[4,64,8,128]{3,2,1,0:T(8,128)S(1)}) %tuple.15, (s32[]{:T(128)}, s32[64,1]{0,1:T(1,128)S(1)}, s32[64,2048]{1,0:T(8,128)S(1)}, bf16[2048,1024]{1,0:T(8,128)(2,1)}, ...), branch_computations={%region_4.5_spmd, %region_5.8_spmd} | conditional | flops 2194280448 | bytes 75088664 | solution.py:89
  215.8 6.5 %copy.49 = bf16[2048,1024]{0,1:T(8,128)(2,1)} copy(bf16[2048,1024]{1,0:T(8,128)(2,1)} %get-tuple-element.66) | data formatting | bytes 8388608 | tf_op jit(solution)/shard_map
  222.3 4.0 %fusion.41 = (bf16[2048,512]{0,1:T(8,128)(2,1)}, bf16[2048,512]{0,1:T(8,128)(2,1)S(1)}) fusion(bf16[2048,1024]{0,1:T(8,128)(2,1)} %copy.49), kind=kLoop, calls=%fused_computation.55 | loop fusion | bytes 8388608 | tf_op jit(solution)/shard_map/cond/branch_1_fun/slice | solution.py:54
  226.3 3.9 %select_reduce_fusion = (f32[4,64,8]{2,1,0:T(8,128)S(1)}, f32[4,64,8,2048]{3,2,1,0:T(8,128)S(1)}) fusion(pred[64,2048]{1,0:T(8,128)(4,1)S(1)} %broadcast_compare_fusion, bf16[2048,4,128,1]{0,2,3,1:T(8,128)(2,1)S(1)} %bitcast.62, bf16[64,4,8,128]{3,2,1,0:T(8,128)(2,1)S(1)} %get-tuple-element.67), kind=kOutput, calls=%fused_computation.2 | convolution fusion | flops 1086322688 | bytes 19537920 | tf_op jit(solution)/shard_map/cond/branch_1_fun/rgjd,ngd->grjn/dot_general | solution.py:56
  230.2 5.0 %fusion.1 = f32[4,64,8]{2,1,0:T(8,128)S(1)} fusion(f32[4,64,8,2048]{3,2,1,0:T(8,128)S(1)} %get-tuple-element.76, f32[4,64,8]{2,1,0:T(8,128)S(1)} %max.2, pred[64,2048]{1,0:T(8,128)(4,1)S(1)} %broadcast_compare_fusion), kind=kLoop, calls=%fused_computation.4 | loop fusion | flops 16775168 | bytes 16924672 | tf_op jit(solution)/shard_map/cond/branch_1_fun/reduce_sum | solution.py:63
  235.3 6.5 %fusion.5 = f32[4,64,8,128]{3,2,1,0:T(8,128)S(1)} fusion(bf16[2048,4,128,1]{0,2,3,1:T(8,128)(2,1)} %bitcast.68, f32[4,64,8,2048]{3,2,1,0:T(8,128)S(1)} %get-tuple-element.76, f32[4,64,8]{2,1,0:T(8,128)S(1)} %max.2, pred[64,2048]{1,0:T(8,128)(4,1)S(1)} %broadcast_compare_fusion, f32[4,64,8,128]{3,2,1,0:T(8,128)S(1)} %get-tuple-element.32, ...), kind=kOutput, calls=%fused_computation.7 | convolution fusion | flops 1091043328 | bytes 21118976 | tf_op jit(solution)/shard_map/cond/branch_1_fun/grjn,ngd->grjd/dot_general | solution.py:64
  243.0 3.4 %collective-permute-start = (bf16[1,64,4096]{2,1,0:T(8,128)(2,1)S(1)}, bf16[1,64,4096]{2,1,0:T(8,128)(2,1)S(1)}, u32[]{:S(2)}, u32[]{:S(2)}) collective-permute-start(bf16[1,64,4096]{2,1,0:T(8,128)(2,1)S(1)} %fusion.32), channel_id=1, source_target_pairs={{480,0},{0,32},{32,64},{64,96},{96,128},{128,160},{160,192},{192,2... | collective-permute-start | bytes 1572872 | tf_op jit(solution)/shard_map/ppermute | solution.py:15
  247.2 51.6 %collective-permute-done = bf16[1,64,4096]{2,1,0:T(8,128)(2,1)S(1)} collective-permute-done((bf16[1,64,4096]{2,1,0:T(8,128)(2,1)S(1)}, bf16[1,64,4096]{2,1,0:T(8,128)(2,1)S(1)}, u32[]{:S(2)}, u32[]{:S(2)}) %collective-permute-start) | collective-permute-done | bytes 524320 | tf_op jit(solution)/shard_map/ppermute | solution.py:15
  298.9 0.8 copy.87
  (37 shorter events, 5.8 us)
Async XLA Ops:
  7.2 6.0 %copy-start = (bf16[1,64,4096]{2,1,0:T(8,128)(2,1)S(1)}, bf16[1,64,4096]{2,1,0:T(8,128)(2,1)}, u32[]{:S(2)}) copy-start(bf16[1,64,4096]{2,1,0:T(8,128)(2,1)} %param.9) | copy-start | bytes 1572868
  7.2 74.1 %all-gather.10.cloned.1.call-start = ((), (), s32[]{:S(2)}) async-start(), calls=%async_computation.2 | async-start | bytes 5406720 | tf_op jit(solution)/shard_map/all_gather | solution.py:76
  7.9 138.3 %all-gather.8.cloned.1.call-start = ((), (), s32[]{:S(2)}) async-start(), calls=%async_computation.1 | async-start | bytes 1081344 | tf_op jit(solution)/shard_map/all_gather | solution.py:82
  8.7 206.9 %all-gather.6.cloned.1.call-start = ((), (), s32[]{:S(2)}) async-start(), calls=%async_computation | async-start | bytes 4325376 | tf_op jit(solution)/shard_map/all_gather | solution.py:86
  87.7 3.7 %copy-start.2 = (bf16[1,64,4096]{2,1,0:T(8,128)(2,1)S(1)}, bf16[1,64,4096]{2,1,0:T(8,128)(2,1)}, u32[]{:S(2)}) copy-start(bf16[1,64,4096]{2,1,0:T(8,128)(2,1)} %param.11) | copy-start | bytes 1572868
  241.9 1.0 copy-start.1
  243.0 55.8 %collective-permute-start = (bf16[1,64,4096]{2,1,0:T(8,128)(2,1)S(1)}, bf16[1,64,4096]{2,1,0:T(8,128)(2,1)S(1)}, u32[]{:S(2)}, u32[]{:S(2)}) collective-permute-start(bf16[1,64,4096]{2,1,0:T(8,128)(2,1)S(1)} %fusion.32), channel_id=1, source_target_pairs={{480,0},{0,32},{32,64},{64,96},{96,128},{128,160},{160,192},{192,2... | collective-permute-start | bytes 1572872 | tf_op jit(solution)/shard_map/ppermute | solution.py:15
Sparse Core Ops, SparseCore 0:
  10.1 71.0 all-gather.9
  83.4 62.7 all-gather.7
  148.9 66.6 all-gather.5
where the time goes:
time: 307 us; the launch traced here: 306 us
  waiting for transfers between devices  238 us (78%)
  matrix products  19 us (6%)
  local copies, waits for them, and re-layouts  18 us (6%)
  between operations  14 us (5%)
  other arithmetic  13.6 us (4%)
  starting transfers between devices  3.49 us (1%)
    all_gather x1, waiting for transfers between devices, local(): lax.all_gather(panel_blocks[0], 'zero', axis=0, tiled=True)  66.1 us
    all_gather x1, waiting for transfers between devices, local(): portion = lax.all_gather(kv_new, 'zero', axis=0, tiled=True)  64.2 us
    all_gather x1, waiting for transfers between devices, local(): cache_portion = lax.all_gather(cached_kv[0], 'zero', axis=0, tiled=True)  54.7 us
    ppermute x1, waiting for transfers between devices, passed_along(): return lax.ppermute(block, axis, route)  51.6 us
    dot_general x2, matrix products, absorb(): jnp.einsum('grjn,ngd->grjd', weights.astype(jnp.bfloat16), value_grid, pr...  8.01 us
    another operation x1, local copies, waits for them, and re-layouts  6.53 us
    dot_general x1, matrix products, local(): jnp.einsum('rsk,skn->rsn', chosen, lax.all_gather(panel_blocks[0], 'zero'...  6.4 us
    reduce_sum x2, other arithmetic, absorb(): new_sum = run_sum * shrink + jnp.sum(weights, axis=-1)  6.31 us
  transfers between devices with their start and end apart: 4, of which 4 were waited for; matrix products, arithmetic and copies ran while one was open for 7% of the time, Pallas kernels for 0%

commit v1 on v0

--- a/solution.py
+++ b/solution.py
@@ -79,7 +79,9 @@
     slot_terms = slot_terms * slot_live[None, :, None]
     summed = slot_terms.reshape(row_count, panels, slot_depth, block_size).sum(axis=2)
     kv_new = summed.reshape(row_count, panels * block_size).astype(jnp.bfloat16)
-    cache_portion = lax.all_gather(cached_kv[0], "zero", axis=0, tiled=True)
+    cache_portion = jnp.concatenate(
+        lax.all_to_all(jnp.stack([cached_kv[0]] * lax.axis_size("zero")), "zero", 0, 0), axis=0
+    )
     softmax_state = absorb(
         initial, cache_portion, jnp.ones((row_count, cache_portion.shape[0]), bool)
     )

time: 307 us -> 256 us (0.83)
  the two profiles are of different devices: /device:TPU:96 before, /device:TPU:67 now
where the time goes in v1:
time: 256 us
  waiting for transfers between devices  181 us (71%)
  matrix products  19 us (7%)
  local copies, waits for them, and re-layouts  18.1 us (7%)
  between operations  14.3 us (6%)
  other arithmetic  13.6 us (5%)
  starting transfers between devices  9.94 us (4%)
    all_gather x1, waiting for transfers between devices, local(): lax.all_gather(panel_blocks[0], 'zero', axis=0, tiled=True)  67.7 us
    ppermute x1, waiting for transfers between devices, passed_along(): return lax.ppermute(block, axis, route)  51.5 us
    all_gather x1, waiting for transfers between devices, local(): portion = lax.all_gather(kv_new, 'zero', axis=0, tiled=True)  31.7 us
    all_to_all x1, waiting for transfers between devices, local(): lax.all_to_all(jnp.stack([cached_kv[0]] * lax.axis_size('zero')), 'zero',...  29.1 us
    dot_general x2, matrix products, absorb(): jnp.einsum('grjn,ngd->grjd', weights.astype(jnp.bfloat16), value_grid, pr...  7.99 us
    all_to_all x1, starting transfers between devices, local(): lax.all_to_all(jnp.stack([cached_kv[0]] * lax.axis_size('zero')), 'zero',...  6.75 us
    another operation x1, local copies, waits for them, and re-layouts  6.53 us
    dot_general x1, matrix products, local(): jnp.einsum('rsk,skn->rsn', chosen, lax.all_gather(panel_blocks[0], 'zero'...  6.41 us
  transfers between devices with their start and end apart: 4, of which 4 were waited for; matrix products, arithmetic and copies ran while one was open for 5% of the time, Pallas kernels for 0%

profile of v1, /device:TPU:67, one launch (start us, length us, event | category | flops | bytes accessed | tf_op | source)
XLA Modules:
  0.0 255.7 jit_solution(1734121734246441163)
XLA Ops:
  8.0 0.8 reshape_squeeze.10
  8.7 0.8 reshape_squeeze.9
  10.3 0.7 mul.79
  11.0 1.1 convert_bitcast_fusion
  13.3 1.1 gather_fusion
  14.4 67.7 %all-gather.6.cloned.1.call-done = bf16[1,160,128,128]{3,2,0,1:T(8,128)(2,1)} async-done(((bf16[1,5,128,128]{3,2,0,1:T(8,128)(2,1)}), bf16[1,160,128,128]{3,2,0,1:T(8,128)(2,1)}) %all-gather.6.cloned.1.call-update) | async-done | bytes 5242896 | tf_op jit(solution)/shard_map/all_gather | solution.py:76
  82.1 6.4 %broadcast_multiply_fusion = f32[160,64,128]{2,1,0:T(8,128)} fusion(f32[160]{0:T(256)S(1)} %reshape.136, bf16[1,160,128,128]{3,2,0,1:T(8,128)(2,1)} %all-gather.6.cloned.1.call-done, bf16[160,64,128]{2,1,0:T(8,128)(2,1)S(1)} %gather_fusion, pred[160]{0:T(512)(128)(4,1)S(1)} %compare_and_fusion), kind=kOutput, calls=%fused_computation.24 | convolution fusion | flops 338165760 | bytes 13108000 | tf_op jit(solution)/shard_map/rsk,skn->rsn/dot_general | solution.py:73
  88.5 3.0 %reduce_sum.38 = bf16[64,8,128]{2,0,1:T(8,128)(2,1)S(1)} reduce(f32[64,8,20,128]{3,0,2,1:T(8,128)} %bitcast.62, f32[]{:T(128)} %constant.28.clone.1), dimensions={2}, to_apply=%region_3.4 | reduce | flops 1245184 | bytes 5373956 | tf_op jit(solution)/shard_map/reduce_sum | solution.py:80
  92.2 1.1 stack.3
  93.3 6.8 %all-to-all-start = ((bf16[32,16,1024]{2,1,0:T(8,128)(2,1)}), bf16[32,16,1024]{2,1,0:T(8,128)(2,1)S(1)}, u32[]{:S(2)}, u32[]{:S(2)}) async-start(bf16[32,16,1024]{2,1,0:T(8,128)(2,1)} %stack.3), calls=%async_computation | async-start | bytes 2097152 | tf_op jit(solution)/shard_map/all_to_all | solution.py:83
  100.2 29.1 %all-to-all-done = bf16[32,16,1024]{2,1,0:T(8,128)(2,1)S(1)} async-done(((bf16[32,16,1024]{2,1,0:T(8,128)(2,1)}), bf16[32,16,1024]{2,1,0:T(8,128)(2,1)S(1)}, u32[]{:S(2)}, u32[]{:S(2)}) %all-to-all-start) | async-done | bytes 1048608 | tf_op jit(solution)/shard_map/all_to_all | solution.py:83
  129.9 0.8 multiply_reduce_fusion
  130.7 1.3 fusion.15
  132.0 1.5 fusion.27
  133.5 31.7 %all-gather.4.cloned.1.call-done = bf16[2048,1024]{1,0:T(8,128)(2,1)} async-done(((bf16[64,1024]{1,0:T(8,128)(2,1)}), bf16[2048,1024]{1,0:T(8,128)(2,1)}) %all-gather.4.cloned.1.call-update) | async-done | bytes 4194320 | tf_op jit(solution)/shard_map/all_gather | solution.py:88
  165.2 26.3 %conditional.1 = ((f32[4,64,8]{2,1,0:T(8,128)S(1)}, f32[4,64,8,128]{3,2,1,0:T(8,128)S(1)})) conditional(s32[]{:T(128)} %convert_element_type.57, (f32[4,64,8]{2,1,0:T(8,128)S(1)}, f32[4,64,8,128]{3,2,1,0:T(8,128)S(1)}) %tuple.15, (s32[]{:T(128)}, s32[64,1]{0,1:T(1,128)S(1)}, s32[64,2048]{1,0:T(8,128)S(1)}, bf16[2048,1024]{1,0:T(8,128)(2,1)}, ...), branch_computations={%region_4.5_spmd, %region_5.8_spmd} | conditional | flops 2194280448 | bytes 75088664 | solution.py:91
  165.4 6.5 %copy.52 = bf16[2048,1024]{0,1:T(8,128)(2,1)} copy(bf16[2048,1024]{1,0:T(8,128)(2,1)} %get-tuple-element.66) | data formatting | bytes 8388608 | tf_op jit(solution)/shard_map
  171.9 4.0 %fusion.41 = (bf16[2048,512]{0,1:T(8,128)(2,1)}, bf16[2048,512]{0,1:T(8,128)(2,1)S(1)}) fusion(bf16[2048,1024]{0,1:T(8,128)(2,1)} %copy.52), kind=kLoop, calls=%fused_computation.55 | loop fusion | bytes 8388608 | tf_op jit(solution)/shard_map/cond/branch_1_fun/slice | solution.py:54
  176.0 3.9 %select_reduce_fusion = (f32[4,64,8]{2,1,0:T(8,128)S(1)}, f32[4,64,8,2048]{3,2,1,0:T(8,128)S(1)}) fusion(pred[64,2048]{1,0:T(8,128)(4,1)S(1)} %broadcast_compare_fusion, bf16[2048,4,128,1]{0,2,3,1:T(8,128)(2,1)S(1)} %bitcast.63, bf16[64,4,8,128]{3,2,1,0:T(8,128)(2,1)S(1)} %get-tuple-element.67), kind=kOutput, calls=%fused_computation.2 | convolution fusion | flops 1086322688 | bytes 19537920 | tf_op jit(solution)/shard_map/cond/branch_1_fun/rgjd,ngd->grjn/dot_general | solution.py:56
  179.8 5.0 %fusion.1 = f32[4,64,8]{2,1,0:T(8,128)S(1)} fusion(f32[4,64,8,2048]{3,2,1,0:T(8,128)S(1)} %get-tuple-element.76, f32[4,64,8]{2,1,0:T(8,128)S(1)} %max.2, pred[64,2048]{1,0:T(8,128)(4,1)S(1)} %broadcast_compare_fusion), kind=kLoop, calls=%fused_computation.4 | loop fusion | flops 16775168 | bytes 16924672 | tf_op jit(solution)/shard_map/cond/branch_1_fun/reduce_sum | solution.py:63
  185.0 6.5 %fusion.5 = f32[4,64,8,128]{3,2,1,0:T(8,128)S(1)} fusion(bf16[2048,4,128,1]{0,2,3,1:T(8,128)(2,1)} %bitcast.69, f32[4,64,8,2048]{3,2,1,0:T(8,128)S(1)} %get-tuple-element.76, f32[4,64,8]{2,1,0:T(8,128)S(1)} %max.2, pred[64,2048]{1,0:T(8,128)(4,1)S(1)} %broadcast_compare_fusion, f32[4,64,8,128]{3,2,1,0:T(8,128)S(1)} %get-tuple-element.32, ...), kind=kOutput, calls=%fused_computation.7 | convolution fusion | flops 1091043328 | bytes 21118976 | tf_op jit(solution)/shard_map/cond/branch_1_fun/grjn,ngd->grjd/dot_general | solution.py:64
  192.7 3.1 %collective-permute-start = (bf16[1,64,4096]{2,1,0:T(8,128)(2,1)S(1)}, bf16[1,64,4096]{2,1,0:T(8,128)(2,1)S(1)}, u32[]{:S(2)}, u32[]{:S(2)}) collective-permute-start(bf16[1,64,4096]{2,1,0:T(8,128)(2,1)S(1)} %fusion.32), channel_id=1, source_target_pairs={{480,0},{0,32},{32,64},{64,96},{96,128},{128,160},{160,192},{192,2... | collective-permute-start | bytes 1572872 | tf_op jit(solution)/shard_map/ppermute | solution.py:15
  196.6 51.5 %collective-permute-done = bf16[1,64,4096]{2,1,0:T(8,128)(2,1)S(1)} collective-permute-done((bf16[1,64,4096]{2,1,0:T(8,128)(2,1)S(1)}, bf16[1,64,4096]{2,1,0:T(8,128)(2,1)S(1)}, u32[]{:S(2)}, u32[]{:S(2)}) %collective-permute-start) | collective-permute-done | bytes 524320 | tf_op jit(solution)/shard_map/ppermute | solution.py:15
  248.1 0.8 copy.90
  (44 shorter events, 6.3 us)
Async XLA Ops:
  7.2 5.2 %copy-start = (bf16[1,64,4096]{2,1,0:T(8,128)(2,1)S(1)}, bf16[1,64,4096]{2,1,0:T(8,128)(2,1)}, u32[]{:S(2)}) copy-start(bf16[1,64,4096]{2,1,0:T(8,128)(2,1)} %param.9) | copy-start | bytes 1572868
  7.2 74.9 %all-gather.6.cloned.1.call-start = ((), (), s32[]{:S(2)}) async-start(), calls=%async_computation.2 | async-start | bytes 5406720 | tf_op jit(solution)/shard_map/all_gather | solution.py:76
  7.9 157.3 %all-gather.4.cloned.1.call-start = ((), (), s32[]{:S(2)}) async-start(), calls=%async_computation.1 | async-start | bytes 4325376 | tf_op jit(solution)/shard_map/all_gather | solution.py:88
  88.5 3.7 %copy-start.5 = (bf16[1,16,1024]{2,1,0:T(8,128)(2,1)S(1)}, bf16[1,16,1024]{2,1,0:T(8,128)(2,1)}, u32[]{:S(2)}) copy-start(bf16[1,16,1024]{2,1,0:T(8,128)(2,1)} %param.12) | copy-start | bytes 98308
  88.5 11.6 %copy-start.4 = (bf16[1,64,4096]{2,1,0:T(8,128)(2,1)S(1)}, bf16[1,64,4096]{2,1,0:T(8,128)(2,1)}, u32[]{:S(2)}) copy-start(bf16[1,64,4096]{2,1,0:T(8,128)(2,1)} %param.11) | copy-start | bytes 1572868
  91.5 37.9 %copy-start.2 = (bf16[64,8,128]{2,0,1:T(8,128)(2,1)}, bf16[64,8,128]{2,0,1:T(8,128)(2,1)S(1)}, u32[]{:S(2)}) copy-start(bf16[64,8,128]{2,0,1:T(8,128)(2,1)S(1)} %reduce_sum.38) | copy-start | bytes 393220
  93.3 36.0 %all-to-all-start = ((bf16[32,16,1024]{2,1,0:T(8,128)(2,1)}), bf16[32,16,1024]{2,1,0:T(8,128)(2,1)S(1)}, u32[]{:S(2)}, u32[]{:S(2)}) async-start(bf16[32,16,1024]{2,1,0:T(8,128)(2,1)} %stack.3), calls=%async_computation | async-start | bytes 2097152 | tf_op jit(solution)/shard_map/all_to_all | solution.py:83
  191.5 1.0 copy-start.1
  191.5 4.2 %copy-start.3 = (bf16[64,8,128]{2,0,1:T(8,128)(2,1)S(1)}, bf16[64,8,128]{2,0,1:T(8,128)(2,1)}, u32[]{:S(2)}) copy-start(bf16[64,8,128]{2,0,1:T(8,128)(2,1)} %copy-done.2) | copy-start | bytes 393220
  192.7 55.4 %collective-permute-start = (bf16[1,64,4096]{2,1,0:T(8,128)(2,1)S(1)}, bf16[1,64,4096]{2,1,0:T(8,128)(2,1)S(1)}, u32[]{:S(2)}, u32[]{:S(2)}) collective-permute-start(bf16[1,64,4096]{2,1,0:T(8,128)(2,1)S(1)} %fusion.32), channel_id=1, source_target_pairs={{480,0},{0,32},{32,64},{64,96},{96,128},{128,160},{160,192},{192,2... | collective-permute-start | bytes 1572872 | tf_op jit(solution)/shard_map/ppermute | solution.py:15
Sparse Core Ops, SparseCore 0:
  10.1 71.9 all-gather.5
  92.4 72.7 all-gather.3
